TPU v7x, 256 devices: a whole 4x4x8 slice. The times are simulated.
256 devices in a mesh: grp: 8 (over x, core), cell: 32 (over y, z).
Axes of the slice: x: 4, y: 4, z: 8, core: 2. Of those that a mesh axis runs over, the one named last changes fastest.
Arguments:
- rhs: float32 [128, 2, 128, 16, 128], P('grp', None, 'cell'), may hold values from -8 to 8
- log_perm: float32 [128, 128, 16, 128], P('grp', 'cell'), may hold values from -1.5 to 1.5
- porosity: float32 [128, 128, 16, 128], P('grp', 'cell'), may hold values from 0.1 to 0.3
- saturation: float32 [128, 128, 16, 128], P('grp', 'cell'), may hold values from 0.2 to 0.8
- pressure: float32 [128, 128, 16, 128], P('grp', 'cell'), may hold values from -6 to 6
- obs_values: float32 [256], replicated, may hold values from -6 to 6
- obs_error: float32 [256], replicated, may hold values from 0.1 to 1
- noise: float32 [128, 256], replicated, may hold values from -6 to 6
- well_cell: int32 [128], replicated, may hold values from 0 to 262143
- obs_well: int32 [256], replicated, may hold values from 0 to 127
Outputs:
- increment: float32 [128, 2, 128, 16, 128], P('grp', None, 'cell')
- log_perm_post: float32 [128, 128, 16, 128], P('grp', 'cell')
- porosity_post: float32 [128, 128, 16, 128], P('grp', 'cell')
All inputs are finite; a program needn't handle non-finite values.
Results may differ from a plain program's by a relative error of at most 0.0003.
Values sent between devices are 32-bit elements; how exact they have to be, the bound alone decides.
No kernel may reach another device: no remote copies, remote signals or barrier semaphores. Data moves between devices by JAX's collectives and lax.ppermute only.
A program may use at most 128 MiB of HBM per device.

v0:
```python
import math
import jax
import jax.numpy as jnp
from jax import lax
from jax.sharding import Mesh
from jax.sharding import PartitionSpec as P

KRYLOV = 4
epsilon = 1e-06
time_step = 0.1
compress = 0.5
inflation = 4.0
CELL = ("cy", "cz")


def cell_sum(values, doubling=False):
    for axis in ("cz", "cy"):
        size = lax.axis_size(axis)
        if not doubling or size & size - 1:
            values = lax.psum(values, axis)
            continue
        step = 1
        while step < size:
            values = values + lax.ppermute(values, axis, [(i, i ^ step) for i in range(size)])
            step *= 2
    return values


def with_halo(block, sides, width):
    for axis, dim in sides:
        count = lax.axis_size(axis[0]) * lax.axis_size(axis[1])
        forward = [(i, i + 1) for i in range(count - 1)]
        backward = [(target, source) for source, target in forward]
        low = lax.ppermute(
            lax.slice_in_dim(block, block.shape[dim] - width, None, axis=dim), axis, forward
        )
        high = lax.ppermute(lax.slice_in_dim(block, 0, width, axis=dim), axis, backward)
        block = jnp.concatenate([low, block, high], axis=dim)
    return block


def mobility(sat_field):
    return sat_field * sat_field + 0.5 * (1.0 - sat_field) * (1.0 - sat_field)


def face_pair(perm_low, perm_high, sat_low, sat_high):
    trans = (
        2.0
        * perm_low
        * perm_high
        / (perm_low + perm_high)
        * (0.5 * (mobility(sat_low) + mobility(sat_high)))
    )
    return (trans, trans * (0.5 * (sat_low + sat_high)))


def plane_faces(perm, sat_field):
    plane_rows = perm.shape[-2]
    plane_cols = perm.shape[-1]
    keep_rows = (
        lax.broadcasted_iota(jnp.int32, (plane_rows, plane_cols), 0) < plane_rows - 1
    ).astype(jnp.float32)
    keep_cols = (
        lax.broadcasted_iota(jnp.int32, (plane_rows, plane_cols), 1) < plane_cols - 1
    ).astype(jnp.float32)
    trans_y, frac_y = face_pair(
        perm, jnp.roll(perm, -1, -2), sat_field, jnp.roll(sat_field, -1, -2)
    )
    trans_z, frac_z = face_pair(
        perm, jnp.roll(perm, -1, -1), sat_field, jnp.roll(sat_field, -1, -1)
    )
    return (trans_y * keep_rows, frac_y * keep_rows, trans_z * keep_cols, frac_z * keep_cols)


def operator(padded, second, coeffs):
    accum, trans_x, frac_x, trans_y, frac_y, trans_z, frac_z = coeffs
    first = padded[..., 1:-1, :, :]
    diff_x = padded[..., 1:, :, :] - padded[..., :-1, :, :]
    diff_y = jnp.roll(first, -1, -2) - first
    diff_z = jnp.roll(first, -1, -1) - first

    def net(coef_x, coef_y, coef_z):
        flow_x = coef_x * diff_x
        flow_y = coef_y * diff_y
        flow_z = coef_z * diff_z
        return (
            flow_x[..., :-1, :, :]
            - flow_x[..., 1:, :, :]
            + (jnp.roll(flow_y, 1, -2) - flow_y)
            + (jnp.roll(flow_z, 1, -1) - flow_z)
        )

    out_pressure = accum * (compress * first + 0.5 * second) + net(trans_x, trans_y, trans_z)
    out_water = accum * second + net(frac_x, frac_y, frac_z)
    return (out_pressure, out_water)


def least_squares(columns, beta):
    rows = [list(column) for column in columns]
    cosines = []
    sines = []
    target = [beta] + [jnp.zeros_like(beta) for column in columns]
    for jdx in range(len(rows)):
        column = rows[jdx]
        for idx in range(jdx):
            upper = cosines[idx] * column[idx] + sines[idx] * column[idx + 1]
            column[idx + 1] = -sines[idx] * column[idx] + cosines[idx] * column[idx + 1]
            column[idx] = upper
        radius = jnp.sqrt(column[jdx] * column[jdx] + column[jdx + 1] * column[jdx + 1])
        cosines.append(column[jdx] / radius)
        sines.append(column[jdx + 1] / radius)
        column[jdx] = radius
        target[jdx + 1] = -sines[jdx] * target[jdx]
        target[jdx] = cosines[jdx] * target[jdx]
    count = len(rows)
    solved = [None] * count
    for jdx in reversed(range(count)):
        partial_sum = target[jdx]
        for idx in range(jdx + 1, count):
            partial_sum = partial_sum - rows[idx][jdx] * solved[idx]
        solved[jdx] = partial_sum / rows[jdx][jdx]
    return solved


def ensemble_weights(predicted, obs_values, obs_error, noise, offset, count):
    members = predicted.shape[0]
    sigma = math.sqrt(inflation) * obs_error
    center = jnp.mean(predicted, axis=0)
    spread = (predicted - center) / (math.sqrt(members - 1.0) * sigma)
    innov = (obs_values + sigma * noise - predicted) / sigma
    own_innov = lax.dynamic_slice_in_dim(innov, offset, count, 0)
    gram = jnp.eye(members, dtype=jnp.float32) + jnp.dot(
        spread, spread.T, precision=lax.Precision.HIGHEST, preferred_element_type=jnp.float32
    )
    cross = jnp.dot(
        spread, own_innov.T, precision=lax.Precision.HIGHEST, preferred_element_type=jnp.float32
    )
    factor = jnp.linalg.cholesky(gram)
    return jax.scipy.linalg.cho_solve((factor, True), cross)


def expand(values):
    return values[:, None, None, None, None]


def inner(left, right):
    return jnp.sum(left * right, axis=(1, 2, 3, 4))


def local(
    rhs, log_perm, porosity, saturation, pressure, obs_values, obs_error, noise, well_cell, obs_well
):
    local_members, slab_x, plane_rows, plane_cols = log_perm.shape
    members = noise.shape[0]
    plane = plane_rows * plane_cols
    cells_dev = slab_x * plane
    slab_index = lax.axis_index("cy") * lax.axis_size("cz") + lax.axis_index("cz")
    slab_count = lax.axis_size("cy") * lax.axis_size("cz")
    count = slab_count
    forward = [(i, i + 1) for i in range(count - 1)]
    backward = [(target, source) for source, target in forward]
    edges = (log_perm, saturation, rhs[:, 0])
    low = lax.ppermute(jnp.stack([field[:, -1:] for field in edges], 1), CELL, forward)
    high = lax.ppermute(jnp.stack([field[:, :1] for field in edges], 1), CELL, backward)
    perm_pad = jnp.exp(jnp.concatenate([low[:, 0], log_perm, high[:, 0]], axis=1))
    sat_pad = jnp.concatenate([low[:, 1], saturation, high[:, 1]], axis=1)
    trans_x, frac_x = face_pair(perm_pad[:, :-1], perm_pad[:, 1:], sat_pad[:, :-1], sat_pad[:, 1:])
    face_pos = lax.broadcasted_iota(jnp.int32, (slab_x + 1, 1, 1), 0)
    keep_face = jnp.where(
        face_pos == 0,
        slab_index > 0,
        jnp.where(face_pos == slab_x, slab_index < slab_count - 1, True),
    ).astype(jnp.float32)
    trans_x = trans_x * keep_face
    frac_x = frac_x * keep_face
    trans_y, frac_y, trans_z, frac_z = plane_faces(perm_pad[:, 1:-1], saturation)
    coeffs = (porosity / time_step, trans_x, frac_x, trans_y, frac_y, trans_z, frac_z)

    def planes(field):
        low = lax.ppermute(field[:, -1:], CELL, forward)
        high = lax.ppermute(field[:, :1], CELL, backward)
        return (low, high)

    def apply(vector, ghosts):
        padded = jnp.concatenate([ghosts[0], vector[:, 0], ghosts[1]], axis=1)
        out_pressure, out_water = operator(padded, vector[:, 1], coeffs)
        return jnp.stack([out_pressure, out_water], 1)

    def scale_planes(ghosts, scale):
        factor = scale[:, None, None, None]
        return (ghosts[0] / factor, ghosts[1] / factor)

    rhs_planes = (low[:, 2], high[:, 2])
    image = apply(rhs, rhs_planes)
    image_planes = planes(image[:, 0])
    reduced = cell_sum(jnp.stack([inner(rhs, rhs), inner(rhs, image)], 0))
    beta = jnp.sqrt(reduced[0] + epsilon)
    basis = [rhs / expand(beta)]
    basis_planes = [scale_planes(rhs_planes, beta)]
    image = image / expand(beta)
    image_planes = scale_planes(image_planes, beta)
    projected = [reduced[1] / (beta * beta)]
    columns = []
    for jdx in range(KRYLOV):
        ortho = image
        ortho_low, ortho_high = image_planes
        for idx in range(jdx + 1):
            ortho = ortho - expand(projected[idx]) * basis[idx]
            factor = projected[idx][:, None, None, None]
            ortho_low = ortho_low - factor * basis_planes[idx][0]
            ortho_high = ortho_high - factor * basis_planes[idx][1]
        ortho_planes = (ortho_low, ortho_high)
        if jdx == KRYLOV - 1:
            height = jnp.sqrt(cell_sum(inner(ortho, ortho)) + epsilon)
            columns.append(projected + [height])
            break
        image = apply(ortho, ortho_planes)
        image_planes = planes(image[:, 0])
        parts = [inner(ortho, ortho)]
        parts += [inner(basis[idx], image) for idx in range(jdx + 1)]
        parts.append(inner(ortho, image))
        reduced = cell_sum(jnp.stack(parts, 0))
        height = jnp.sqrt(reduced[0] + epsilon)
        columns.append(projected + [height])
        basis.append(ortho / expand(height))
        basis_planes.append(scale_planes(ortho_planes, height))
        image = image / expand(height)
        image_planes = scale_planes(image_planes, height)
        projected = [reduced[1 + idx] / height for idx in range(jdx + 1)]
        projected.append(reduced[jdx + 2] / (height * height))
    solved = least_squares(columns, beta)
    increment = expand(solved[0]) * basis[0]
    for jdx in range(1, KRYLOV):
        increment = increment + expand(solved[jdx]) * basis[jdx]
    cells = jnp.take(well_cell, obs_well)
    wells = well_cell.shape[0]
    component = (jnp.arange(obs_well.shape[0], dtype=jnp.int32) >= wells).astype(jnp.int32)
    slab_row = cells // plane - slab_index * slab_x
    inside = (slab_row >= 0) & (slab_row < slab_x)
    rows = 2 * slab_x * plane_rows
    row = component * (slab_x * plane_rows) + slab_row * plane_rows + cells % plane // plane_cols
    col_z = cells % plane_cols
    state = jnp.stack([pressure + increment[:, 0], saturation + increment[:, 1]], 1)
    table = state.reshape(local_members * rows, plane_cols)
    pick_z = lax.broadcasted_iota(jnp.int32, (plane_cols, cells.shape[0]), 0) == col_z[None, :]
    by_row = jnp.dot(
        table,
        pick_z.astype(jnp.float32),
        precision=lax.Precision.HIGHEST,
        preferred_element_type=jnp.float32,
    )
    pick_row = (
        lax.broadcasted_iota(jnp.int32, (rows, cells.shape[0]), 0) == row[None, :]
    ) & inside[None, :]
    picked = jnp.sum(
        by_row.reshape(local_members, rows, cells.shape[0]) * pick_row.astype(jnp.float32)[None],
        axis=1,
    )
    slab_pred = cell_sum(picked, doubling=True)
    predicted = lax.all_gather(slab_pred, "grp", axis=0, tiled=True)
    params = jnp.stack([log_perm, porosity], 1).reshape(local_members, 2 * cells_dev)
    offset = lax.axis_index("grp") * local_members
    own_columns = ensemble_weights(predicted, obs_values, obs_error, noise, offset, local_members)
    scale_factor = 1.0 / math.sqrt(members - 1.0)
    scaled = params * scale_factor
    update = jnp.dot(
        own_columns.T,
        lax.all_gather(scaled, "grp", axis=0, tiled=True),
        precision=lax.Precision.HIGHEST,
        preferred_element_type=jnp.float32,
    )
    posterior = params + update
    posterior = posterior.reshape(local_members, 2, slab_x, plane_rows, plane_cols)
    return (increment, posterior[:, 0], posterior[:, 1])


def split_mesh(mesh):
    devices = mesh.devices
    groups, slabs = devices.shape
    along_z = len({device.coords[2] for device in devices[0]})
    return Mesh(devices.reshape(groups, slabs // along_z, along_z), ("grp", "cy", "cz"))


def solution(mesh):
    mesh = split_mesh(mesh)
    in_specs = (
        P("grp", None, CELL, None, None),
        P("grp", CELL, None, None),
        P("grp", CELL, None, None),
        P("grp", CELL, None, None),
        P("grp", CELL, None, None),
        P(),
        P(),
        P(),
        P(),
        P(),
    )
    out_specs = (
        P("grp", None, CELL, None, None),
        P("grp", CELL, None, None),
        P("grp", CELL, None, None),
    )
    return jax.shard_map(local, mesh=mesh, in_specs=in_specs, out_specs=out_specs, check_vma=False)
```

profile of v0, /device:TPU:1, one launch (start us, length us, event | category | flops | bytes accessed | tf_op | source)
XLA Modules:
  0.0 307.5 jit_solution(6333934453051698767)
XLA Ops:
  13.3 5.0 %collective-permute-start = (f32[16,3,1,16,128]{4,3,0,2,1:T(8,128)}, f32[16,3,1,16,128]{4,3,0,2,1:T(8,128)S(1)}, u32[]{:S(2)}, u32[]{:S(2)}) collective-permute-start(f32[16,3,1,16,128]{4,3,0,2,1:T(8,128)} %pad_maximum_fusion.12), channel_id=1, source_target_pairs={{0,1},{1,2},{2,3},{3,4},{4,5},{5,6},{6,7},{7,8},{8,9},{9,10},{10,1... | collective-permute-start | bytes 1179656 | tf_op jit(solution)/shard_map/ppermute | solution.py:163
  20.8 1.6 bitcast_multiply_fusion
  22.6 1.9 gather_fusion
  31.0 1.6 fusion.94
  34.1 19.3 %psum.70 = f32[2,16]{1,0:T(2,128)S(1)} all-reduce(f32[2,16]{1,0:T(2,128)S(1)} %pad_maximum_fusion.16), channel_id=1, replica_groups=mesh['grp'=8,'cy'=4,'cz'=8] {'cz'}, use_global_device_ids=true, to_apply=%region_2.3 | all-reduce | flops 32 | bytes 256 | tf_op jit(solution)/shard_map/psum | solution.py:20
  53.5 10.3 %psum.71 = f32[2,16]{1,0:T(2,128)S(1)} all-reduce(f32[2,16]{1,0:T(2,128)S(1)} %psum.70), channel_id=1, replica_groups=mesh['grp'=8,'cy'=4,'cz'=8] {'cy'}, use_global_device_ids=true, to_apply=%region_3.4 | all-reduce | flops 32 | bytes 256 | tf_op jit(solution)/shard_map/psum | solution.py:20
  65.8 4.0 %collective-permute-start.3 = (f32[16,1,16,128]{3,2,1,0:T(8,128)S(1)}, f32[16,1,16,128]{3,2,1,0:T(8,128)S(1)}, u32[]{:S(2)}, u32[]{:S(2)}) collective-permute-start(f32[16,1,16,128]{3,2,1,0:T(8,128)S(1)} %get-tuple-element.72), channel_id=1, source_target_pairs={{0,1},{1,2},{2,3},{3,4},{4,5},{5,6},{6,7},{7,8},{8,9},{9,10},{10,1... | collective-permute-start | bytes 393224 | tf_op jit(solution)/shard_map/ppermute | solution.py:180
  69.8 2.0 multiply_multiply_fusion.10
  76.6 14.2 %psum.72 = f32[3,16]{1,0:T(4,128)S(1)} all-reduce(f32[3,16]{1,0:T(4,128)S(1)} %pad_maximum_fusion.14), channel_id=1, replica_groups=mesh['grp'=8,'cy'=4,'cz'=8] {'cz'}, use_global_device_ids=true, to_apply=%region_7.8 | all-reduce | flops 48 | bytes 384 | tf_op jit(solution)/shard_map/psum | solution.py:20
  90.9 6.0 %psum.73 = f32[3,16]{1,0:T(4,128)S(1)} all-reduce(f32[3,16]{1,0:T(4,128)S(1)} %psum.72), channel_id=1, replica_groups=mesh['grp'=8,'cy'=4,'cz'=8] {'cy'}, use_global_device_ids=true, to_apply=%region_8.9 | all-reduce | flops 48 | bytes 384 | tf_op jit(solution)/shard_map/psum | solution.py:20
  97.4 2.6 multiply_subtract_fusion.1
  101.7 4.2 %collective-permute-start.5 = (f32[16,1,16,128]{3,2,1,0:T(8,128)S(1)}, f32[16,1,16,128]{3,2,1,0:T(8,128)S(1)}, u32[]{:S(2)}, u32[]{:S(2)}) collective-permute-start(f32[16,1,16,128]{3,2,1,0:T(8,128)S(1)} %get-tuple-element.70), channel_id=1, source_target_pairs={{0,1},{1,2},{2,3},{3,4},{4,5},{5,6},{6,7},{7,8},{8,9},{9,10},{10,1... | collective-permute-start | bytes 393224 | tf_op jit(solution)/shard_map/ppermute | solution.py:180
  105.9 2.0 multiply_multiply_fusion.9
  112.2 14.7 %psum.74 = f32[4,16]{1,0:T(4,128)} all-reduce(f32[4,16]{1,0:T(4,128)S(1)} %pad_maximum_fusion.15), channel_id=1, replica_groups=mesh['grp'=8,'cy'=4,'cz'=8] {'cz'}, use_global_device_ids=true, to_apply=%region_13.14 | all-reduce | flops 64 | bytes 512 | tf_op jit(solution)/shard_map/psum | solution.py:20
  126.9 7.4 %psum.75 = f32[4,16]{1,0:T(4,128)} all-reduce(f32[4,16]{1,0:T(4,128)} %psum.74), channel_id=1, replica_groups=mesh['grp'=8,'cy'=4,'cz'=8] {'cy'}, use_global_device_ids=true, to_apply=%region_14.15 | all-reduce | flops 64 | bytes 512 | tf_op jit(solution)/shard_map/psum | solution.py:20
  136.1 2.4 copy_subtract_fusion
  140.3 4.0 %collective-permute-start.7 = (f32[16,1,16,128]{3,2,1,0:T(8,128)S(1)}, f32[16,1,16,128]{3,2,1,0:T(8,128)S(1)}, u32[]{:S(2)}, u32[]{:S(2)}) collective-permute-start(f32[16,1,16,128]{3,2,1,0:T(8,128)S(1)} %get-tuple-element.68), channel_id=1, source_target_pairs={{0,1},{1,2},{2,3},{3,4},{4,5},{5,6},{6,7},{7,8},{8,9},{9,10},{10,1... | collective-permute-start | bytes 393224 | tf_op jit(solution)/shard_map/ppermute | solution.py:180
  149.6 14.1 %psum.76 = f32[5,16]{1,0:T(8,128)S(1)} all-reduce(f32[5,16]{1,0:T(8,128)S(1)} %stack.169), channel_id=1, replica_groups=mesh['grp'=8,'cy'=4,'cz'=8] {'cz'}, use_global_device_ids=true, to_apply=%region_20.21 | all-reduce | flops 80 | bytes 640 | tf_op jit(solution)/shard_map/psum | solution.py:20
  163.7 7.9 %psum.77 = f32[5,16]{1,0:T(8,128)S(1)} all-reduce(f32[5,16]{1,0:T(8,128)S(1)} %psum.76), channel_id=1, replica_groups=mesh['grp'=8,'cy'=4,'cz'=8] {'cy'}, use_global_device_ids=true, to_apply=%region_21.22 | all-reduce | flops 80 | bytes 640 | tf_op jit(solution)/shard_map/psum | solution.py:20
  171.7 2.3 multiply_reduce_fusion.1
  174.0 12.3 %psum.78 = f32[16]{0:T(128)S(1)} all-reduce(f32[16]{0:T(128)S(1)} %multiply_reduce_fusion.1), channel_id=1, replica_groups=mesh['grp'=8,'cy'=4,'cz'=8] {'cz'}, use_global_device_ids=true, to_apply=%region_23.24 | all-reduce | flops 16 | bytes 128 | tf_op jit(solution)/shard_map/psum | solution.py:20
  186.3 6.1 %psum.79 = f32[16]{0:T(128)S(1)} all-reduce(f32[16]{0:T(128)S(1)} %psum.78), channel_id=1, replica_groups=mesh['grp'=8,'cy'=4,'cz'=8] {'cy'}, use_global_device_ids=true, to_apply=%region_24.25 | all-reduce | flops 16 | bytes 128 | tf_op jit(solution)/shard_map/psum | solution.py:20
  192.5 2.1 multiply_add_fusion
  197.7 2.5 collective-permute-done.8
  200.1 3.5 %collective-permute-done.9 = f32[16,256]{1,0:T(8,128)S(1)} collective-permute-done((f32[16,256]{1,0:T(8,128)S(1)}, f32[16,256]{1,0:T(8,128)S(1)}, u32[]{:S(2)}, u32[]{:S(2)}) %collective-permute-start.9) | collective-permute-done | bytes 16416 | tf_op jit(solution)/shard_map/ppermute | solution.py:24
  203.7 2.3 collective-permute-start.10
  205.9 4.4 %collective-permute-done.10 = f32[16,256]{1,0:T(8,128)S(1)} collective-permute-done((f32[16,256]{1,0:T(8,128)S(1)}, f32[16,256]{1,0:T(8,128)S(1)}, u32[]{:S(2)}, u32[]{:S(2)}) %collective-permute-start.10) | collective-permute-done | bytes 16416 | tf_op jit(solution)/shard_map/ppermute | solution.py:24
  213.8 3.2 %collective-permute-done.12 = f32[16,256]{1,0:T(8,128)S(1)} collective-permute-done((f32[16,256]{1,0:T(8,128)S(1)}, f32[16,256]{1,0:T(8,128)S(1)}, u32[]{:S(2)}, u32[]{:S(2)}) %collective-permute-start.12) | collective-permute-done | bytes 16416 | tf_op jit(solution)/shard_map/ppermute | solution.py:24
  217.0 50.4 %all_gather.6 = f32[128,256]{1,0:T(8,128)S(1)} all-gather(f32[16,256]{1,0:T(8,128)S(1)} %add.480), channel_id=1, replica_groups=mesh['grp'=8,'cy'=4,'cz'=8] {'grp'}, dimensions={0}, use_global_device_ids=true | all-gather | bytes 147456 | tf_op jit(solution)/shard_map/all_gather | solution.py:260
  267.9 11.7 %cholesky.17 = f32[128,128]{1,0:T(8,128)S(1)} custom-call(f32[128,128]{1,0:T(8,128)S(1)} %fusion.71), custom_call_target="Cholesky" | custom-call | tf_op jit(solution)/shard_map/jit(cholesky)/cholesky | solution.py:138
  280.9 9.8 %custom-call.10 = f32[1,128,128]{1,2,0:T(8,128)S(1)} custom-call(f32[1,128,128]{2,1,0:T(8,128)S(1)} %fusion.65), custom_call_target="InvertDiagBlocksLowerTriangular" | custom-call | tf_op jit(solution)/shard_map/jit(_cho_solve)/triangular_solve | solution.py:139
  292.3 7.1 %fusion = f32[2,8,128,128]{3,1,2,0:T(8,128)S(1)} fusion(f32[128,16]{1,0:T(8,128)S(1)} %fusion.66, f32[128,16384]{1,0:T(8,128)} %all-gather.2.cloned.1.call-done, f32[2,8,128,128]{3,2,1,0:T(8,128)S(1)} %bitcast.504), kind=kOutput, calls=%fused_computation.3 | convolution fusion | flops 402915328 | bytes 10493952 | tf_op jit(solution)/shard_map/dot_general | solution.py:266
  (257 shorter events, 49.3 us)
Async XLA Ops:
  7.2 19.2 %copy-start.2 = (f32[16,2,4,16,128]{4,3,2,1,0:T(8,128)S(1)}, f32[16,2,4,16,128]{4,3,2,1,0:T(8,128)}, u32[]{:S(2)}) copy-start(f32[16,2,4,16,128]{4,3,2,1,0:T(8,128)} %param.10) | copy-start | bytes 3145732
  7.2 18.9 %copy-start.3 = (f32[16,4,16,128]{3,2,1,0:T(8,128)S(1)}, f32[16,4,16,128]{3,2,1,0:T(8,128)}, u32[]{:S(2)}) copy-start(f32[16,4,16,128]{3,2,1,0:T(8,128)} %param.13) | copy-start | bytes 1572868
  7.2 285.1 %all-gather.2.cloned.1.call-start = ((), (), s32[]{:S(2)}) async-start(), calls=%async_computation | async-start | bytes 9437184 | tf_op jit(solution)/shard_map/all_gather | solution.py:268
  11.3 15.3 %collective-permute-start.1 = (f32[16,3,1,16,128]{4,3,0,2,1:T(8,128)}, f32[16,3,1,16,128]{4,3,0,2,1:T(8,128)S(1)}, u32[]{:S(2)}, u32[]{:S(2)}) collective-permute-start(f32[16,3,1,16,128]{4,3,0,2,1:T(8,128)} %pad_maximum_fusion.13), channel_id=1, source_target_pairs={{1,0},{2,1},{3,2},{4,3},{5,4},{6,5},{7,6},{8,7},{9,8},{10,9},{11,1... | collective-permute-start | bytes 1179656 | tf_op jit(solution)/shard_map/ppermute | solution.py:164
  13.3 13.3 %collective-permute-start = (f32[16,3,1,16,128]{4,3,0,2,1:T(8,128)}, f32[16,3,1,16,128]{4,3,0,2,1:T(8,128)S(1)}, u32[]{:S(2)}, u32[]{:S(2)}) collective-permute-start(f32[16,3,1,16,128]{4,3,0,2,1:T(8,128)} %pad_maximum_fusion.12), channel_id=1, source_target_pairs={{0,1},{1,2},{2,3},{3,4},{4,5},{5,6},{6,7},{7,8},{8,9},{9,10},{10,1... | collective-permute-start | bytes 1179656 | tf_op jit(solution)/shard_map/ppermute | solution.py:163
  25.8 80.1 %copy-start.43 = (f32[128]{0:T(128)}, f32[128]{0:T(128)S(1)}, u32[]{:S(2)}) copy-start(f32[128]{0:T(128)S(1)} %compare_convert_fusion) | copy-start | bytes 1540
  25.8 80.1 %copy-start.44 = (f32[16]{0:T(128)}, f32[16]{0:T(128)S(1)}, u32[]{:S(2)}) copy-start(f32[16]{0:T(128)S(1)} %compare_convert_fusion.1) | copy-start | bytes 196
  33.9 41.9 %copy-start.5 = (f32[16,1,4,16,128]{4,3,2,0,1:T(8,128)}, f32[16,1,4,16,128]{4,3,2,0,1:T(8,128)S(1)}, u32[]{:S(2)}) copy-start(f32[16,1,4,16,128]{4,3,2,0,1:T(8,128)S(1)} %fusion.45) | copy-start | bytes 1572868
  63.7 33.1 %copy-start.47 = (f32[2,16]{1,0:T(2,128)}, f32[2,16]{1,0:T(2,128)S(1)}, u32[]{:S(2)}) copy-start(f32[2,16]{1,0:T(2,128)S(1)} %psum.71) | copy-start | bytes 388
  64.4 9.1 %collective-permute-start.2 = (f32[16,1,16,128]{3,2,1,0:T(8,128)S(1)}, f32[16,1,16,128]{3,2,1,0:T(8,128)S(1)}, u32[]{:S(2)}, u32[]{:S(2)}) collective-permute-start(f32[16,1,16,128]{3,2,1,0:T(8,128)S(1)} %get-tuple-element.71), channel_id=1, source_target_pairs={{1,0},{2,1},{3,2},{4,3},{5,4},{6,5},{7,6},{8,7},{9,8},{10,9},{11,1... | collective-permute-start | bytes 393224 | tf_op jit(solution)/shard_map/ppermute | solution.py:181
  65.8 7.7 %collective-permute-start.3 = (f32[16,1,16,128]{3,2,1,0:T(8,128)S(1)}, f32[16,1,16,128]{3,2,1,0:T(8,128)S(1)}, u32[]{:S(2)}, u32[]{:S(2)}) collective-permute-start(f32[16,1,16,128]{3,2,1,0:T(8,128)S(1)} %get-tuple-element.72), channel_id=1, source_target_pairs={{0,1},{1,2},{2,3},{3,4},{4,5},{5,6},{6,7},{7,8},{8,9},{9,10},{10,1... | collective-permute-start | bytes 393224 | tf_op jit(solution)/shard_map/ppermute | solution.py:180
  100.4 8.0 %collective-permute-start.4 = (f32[16,1,16,128]{3,2,1,0:T(8,128)S(1)}, f32[16,1,16,128]{3,2,1,0:T(8,128)S(1)}, u32[]{:S(2)}, u32[]{:S(2)}) collective-permute-start(f32[16,1,16,128]{3,2,1,0:T(8,128)S(1)} %get-tuple-element.69), channel_id=1, source_target_pairs={{1,0},{2,1},{3,2},{4,3},{5,4},{6,5},{7,6},{8,7},{9,8},{10,9},{11,1... | collective-permute-start | bytes 393224 | tf_op jit(solution)/shard_map/ppermute | solution.py:181
  101.7 6.7 %collective-permute-start.5 = (f32[16,1,16,128]{3,2,1,0:T(8,128)S(1)}, f32[16,1,16,128]{3,2,1,0:T(8,128)S(1)}, u32[]{:S(2)}, u32[]{:S(2)}) collective-permute-start(f32[16,1,16,128]{3,2,1,0:T(8,128)S(1)} %get-tuple-element.70), channel_id=1, source_target_pairs={{0,1},{1,2},{2,3},{3,4},{4,5},{5,6},{6,7},{7,8},{8,9},{9,10},{10,1... | collective-permute-start | bytes 393224 | tf_op jit(solution)/shard_map/ppermute | solution.py:180
  138.9 7.2 %collective-permute-start.6 = (f32[16,1,16,128]{3,2,1,0:T(8,128)S(1)}, f32[16,1,16,128]{3,2,1,0:T(8,128)S(1)}, u32[]{:S(2)}, u32[]{:S(2)}) collective-permute-start(f32[16,1,16,128]{3,2,1,0:T(8,128)S(1)} %get-tuple-element.67), channel_id=1, source_target_pairs={{1,0},{2,1},{3,2},{4,3},{5,4},{6,5},{7,6},{8,7},{9,8},{10,9},{11,1... | collective-permute-start | bytes 393224 | tf_op jit(solution)/shard_map/ppermute | solution.py:181
  140.3 5.9 %collective-permute-start.7 = (f32[16,1,16,128]{3,2,1,0:T(8,128)S(1)}, f32[16,1,16,128]{3,2,1,0:T(8,128)S(1)}, u32[]{:S(2)}, u32[]{:S(2)}) collective-permute-start(f32[16,1,16,128]{3,2,1,0:T(8,128)S(1)} %get-tuple-element.68), channel_id=1, source_target_pairs={{0,1},{1,2},{2,3},{3,4},{4,5},{5,6},{6,7},{7,8},{8,9},{9,10},{10,1... | collective-permute-start | bytes 393224 | tf_op jit(solution)/shard_map/ppermute | solution.py:180
  148.2 44.2 %copy-start.42 = (f32[4,16]{1,0:T(4,128)S(1)}, f32[4,16]{1,0:T(4,128)}, u32[]{:S(2)}) copy-start(f32[4,16]{1,0:T(4,128)} %psum.75) | copy-start | bytes 772
  148.2 44.2 %copy-start.46 = (f32[3,16]{1,0:T(4,128)S(1)}, f32[3,16]{1,0:T(4,128)}, u32[]{:S(2)}) copy-start(f32[3,16]{1,0:T(4,128)} %copy-done.45) | copy-start | bytes 580
  148.2 44.2 %copy-start.48 = (f32[2,16]{1,0:T(2,128)S(1)}, f32[2,16]{1,0:T(2,128)}, u32[]{:S(2)}) copy-start(f32[2,16]{1,0:T(2,128)} %copy-done.47) | copy-start | bytes 388
  148.2 44.2 %copy-start.50 = (f32[16]{0:T(128)S(1)}, f32[16]{0:T(128)}, u32[]{:S(2)}) copy-start(f32[16]{0:T(128)} %copy-done.49) | copy-start | bytes 196
  148.2 44.2 %copy-start.52 = (f32[16]{0:T(128)S(1)}, f32[16]{0:T(128)}, u32[]{:S(2)}) copy-start(f32[16]{0:T(128)} %copy-done.51) | copy-start | bytes 196
  148.2 44.2 %copy-start.55 = (f32[16]{0:T(128)S(1)}, f32[16]{0:T(128)}, u32[]{:S(2)}) copy-start(f32[16]{0:T(128)} %get-tuple-element.97) | copy-start | bytes 196
  173.9 22.5 %copy-start.41 = (f32[128,256]{1,0:T(8,128)S(1)}, f32[128,256]{1,0:T(8,128)}, u32[]{:S(2)}) copy-start(f32[128,256]{1,0:T(8,128)} %fusion.60) | copy-start | bytes 393220
  174.0 22.5 %copy-start.54 = (s32[256]{0:T(256)S(1)}, s32[256]{0:T(256)}, u32[]{:S(2)}) copy-start(s32[256]{0:T(256)} %get-tuple-element.15) | copy-start | bytes 3076
  174.0 39.9 %copy-start.56 = (f32[256]{0:T(256)S(1)}, f32[256]{0:T(256)}, u32[]{:S(2)}) copy-start(f32[256]{0:T(256)} %param.16) | copy-start | bytes 3076
  174.0 116.8 %copy-start.57 = (f32[256]{0:T(256)S(1)}, f32[256]{0:T(256)}, u32[]{:S(2)}) copy-start(f32[256]{0:T(256)} %param.15) | copy-start | bytes 3076
  194.6 97.7 %copy-start.24 = (f32[16,2,4,16,128]{4,3,2,1,0:T(8,128)S(1)}, f32[16,2,4,16,128]{4,3,2,1,0:T(8,128)}, u32[]{:S(2)}) copy-start(f32[16,2,4,16,128]{4,3,2,1,0:T(8,128)} %copy-done.23) | copy-start | bytes 3145732
  197.5 2.7 collective-permute-start.8
  200.1 3.5 %collective-permute-start.9 = (f32[16,256]{1,0:T(8,128)S(1)}, f32[16,256]{1,0:T(8,128)S(1)}, u32[]{:S(2)}, u32[]{:S(2)}) collective-permute-start(f32[16,256]{1,0:T(8,128)S(1)} %add.476), channel_id=1, source_target_pairs={{0,2},{1,3},{2,0},{3,1},{4,6},{5,7},{6,4},{7,5},{8,10},{9,11},{10,... | collective-permute-start | bytes 49160 | tf_op jit(solution)/shard_map/ppermute | solution.py:24
  203.7 6.7 %collective-permute-start.10 = (f32[16,256]{1,0:T(8,128)S(1)}, f32[16,256]{1,0:T(8,128)S(1)}, u32[]{:S(2)}, u32[]{:S(2)}) collective-permute-start(f32[16,256]{1,0:T(8,128)S(1)} %add.477), channel_id=1, source_target_pairs={{0,4},{1,5},{2,6},{3,7},{4,0},{5,1},{6,2},{7,3},{8,12},{9,13},{10,... | collective-permute-start | bytes 49160 | tf_op jit(solution)/shard_map/ppermute | solution.py:24
  210.3 2.6 collective-permute-start.11
  212.9 4.1 %collective-permute-start.12 = (f32[16,256]{1,0:T(8,128)S(1)}, f32[16,256]{1,0:T(8,128)S(1)}, u32[]{:S(2)}, u32[]{:S(2)}) collective-permute-start(f32[16,256]{1,0:T(8,128)S(1)} %add.479), channel_id=1, source_target_pairs={{0,16},{8,24},{16,0},{24,8},{1,17},{9,25},{17,1},{25,9},{2,18},{10... | collective-permute-start | bytes 49160 | tf_op jit(solution)/shard_map/ppermute | solution.py:24
  267.4 33.3 %copy-start.1 = (s32[128]{0:T(128)S(1)}, s32[128]{0:T(128)}, u32[]{:S(2)}) copy-start(s32[128]{0:T(128)} %param.18) | copy-start | bytes 1540
  (40 other events, 284.2 us)
Sparse Core Ops, SparseCore 0:
  22.6 56.6 all-gather.1
where the time goes:
time: 308 us
  blocking collectives  163 us (53%)
  other arithmetic  64.7 us (21%)
  starting transfers between devices  27.4 us (9%)
  between operations  15.4 us (5%)
  waiting for transfers between devices  15 us (5%)
  local copies, waits for them, and re-layouts  12.4 us (4%)
  matrix products  9.87 us (3%)
    psum x10, blocking collectives, cell_sum(): values = lax.psum(values, axis)  112 us
    all_gather x1, blocking collectives, local(): predicted = lax.all_gather(slab_pred, 'grp', axis=0, tiled=True)  50.4 us
    ppermute x5, waiting for transfers between devices, cell_sum(): lax.ppermute(values, axis, [(i, i ^ step) for i in range(size)])  14.8 us
    another operation x3, other arithmetic, ensemble_weights(): factor = jnp.linalg.cholesky(gram)  12.4 us
    ppermute x3, starting transfers between devices, planes(): low = lax.ppermute(field[:, -1:], CELL, forward)  12.2 us
    another operation x2, other arithmetic, ensemble_weights(): return jax.scipy.linalg.cho_solve((factor, True), cross)  10.5 us
    mul x5, other arithmetic, net(): flow_z = coef_z * diff_z  7.78 us
    dot_general x1, matrix products, local(): jnp.dot(own_columns.T, lax.all_gather(scaled, 'grp', axis=0, tiled=True),...  7.11 us
  transfers between devices with their start and end apart: 14, of which 6 were waited for; matrix products, arithmetic and copies ran while one was open for 24% of the time, Pallas kernels for 0%

commit v1 on v0

--- a/solution.py
+++ b/solution.py
@@ -11,6 +11,19 @@
 compress = 0.5
 inflation = 4.0
 CELL = ("cy", "cz")
+
+
+def collect(x, axis, dim):
+    ways = lax.axis_size(axis)
+    up = [(d, (d + 1) % ways) for d in range(ways)]
+    down = [(d, (d - 1) % ways) for d in range(ways)]
+    earlier, later = ([x], [x])
+    for _ in range(ways // 2):
+        earlier.append(lax.ppermute(earlier[-1], axis, up))
+    for _ in range((ways - 1) // 2):
+        later.append(lax.ppermute(later[-1], axis, down))
+    line = jnp.concatenate([*earlier[::-1], *later[1:]], axis=dim)
+    return jnp.roll(line, (lax.axis_index(axis) - ways // 2) * x.shape[dim], axis=dim)
 
 
 def cell_sum(values, doubling=False):
@@ -257,7 +270,7 @@
         axis=1,
     )
     slab_pred = cell_sum(picked, doubling=True)
-    predicted = lax.all_gather(slab_pred, "grp", axis=0, tiled=True)
+    predicted = collect(slab_pred, "grp", 0)
     params = jnp.stack([log_perm, porosity], 1).reshape(local_members, 2 * cells_dev)
     offset = lax.axis_index("grp") * local_members
     own_columns = ensemble_weights(predicted, obs_values, obs_error, noise, offset, local_members)

time: 308 us -> 313 us (1.016); the launches traced: 308 us -> 309 us
  blocking collectives: 163 us -> 112 us
  starting transfers between devices: 27.4 us -> 75.1 us
  waiting for transfers between devices: 15 us -> 18.8 us
    all_gather x1 -> x0, blocking collectives: 50.4 us -> none  [local(): predicted = lax.all_gather(slab_pred, 'grp', axis=0, tiled=True)]
    ppermute x0 -> x7, starting transfers between devices: none -> 47.7 us  [the longest x4 44.4 us: collect(): earlier.append(lax.ppermute(earlier[-1], axis, up))]
    ppermute x0 -> x7, waiting for transfers between devices: none -> 3.75 us  [the longest x4 2.93 us: collect(): earlier.append(lax.ppermute(earlier[-1], axis, up))]
  transfers between devices with their start and end apart: 14 -> 21, of which waited for: 6 -> 13; matrix products, arithmetic and copies ran while one was open for 24% -> 24% of each run, Pallas kernels for 0% -> 0%
where the time goes in v1:
time: 313 us; the launch traced here: 309 us
  blocking collectives  112 us (36%)
  starting transfers between devices  75.1 us (24%)
  other arithmetic  64.8 us (21%)
  waiting for transfers between devices  18.8 us (6%)
  between operations  15.5 us (5%)
  local copies, waits for them, and re-layouts  12.5 us (4%)
  matrix products  9.88 us (3%)
    psum x10, blocking collectives, cell_sum(): values = lax.psum(values, axis)  112 us
    ppermute x4, starting transfers between devices, collect(): earlier.append(lax.ppermute(earlier[-1], axis, up))  44.4 us
    ppermute x5, waiting for transfers between devices, cell_sum(): lax.ppermute(values, axis, [(i, i ^ step) for i in range(size)])  14.8 us
    another operation x3, other arithmetic, ensemble_weights(): factor = jnp.linalg.cholesky(gram)  12.4 us
    ppermute x3, starting transfers between devices, planes(): low = lax.ppermute(field[:, -1:], CELL, forward)  12.2 us
    another operation x2, other arithmetic, ensemble_weights(): return jax.scipy.linalg.cho_solve((factor, True), cross)  10.5 us
    mul x5, other arithmetic, net(): flow_z = coef_z * diff_z  7.72 us
    dot_general x1, matrix products, local(): jnp.dot(own_columns.T, lax.all_gather(scaled, 'grp', axis=0, tiled=True),...  7.11 us
  transfers between devices with their start and end apart: 21, of which 13 were waited for; matrix products, arithmetic and copies ran while one was open for 24% of the time, Pallas kernels for 0%

profile of v1, /device:TPU:1, one launch (start us, length us, event | category | flops | bytes accessed | tf_op | source)
XLA Modules:
  0.0 308.9 jit_solution(1426688836292358365)
XLA Ops:
  13.3 5.0 %collective-permute-start = (f32[16,3,1,16,128]{4,3,0,2,1:T(8,128)}, f32[16,3,1,16,128]{4,3,0,2,1:T(8,128)S(1)}, u32[]{:S(2)}, u32[]{:S(2)}) collective-permute-start(f32[16,3,1,16,128]{4,3,0,2,1:T(8,128)} %pad_maximum_fusion.12), channel_id=1, source_target_pairs={{0,1},{1,2},{2,3},{3,4},{4,5},{5,6},{6,7},{7,8},{8,9},{9,10},{10,1... | collective-permute-start | bytes 1179656 | tf_op jit(solution)/shard_map/ppermute | solution.py:176
  34.1 19.3 %psum.70 = f32[2,16]{1,0:T(2,128)S(1)} all-reduce(f32[2,16]{1,0:T(2,128)S(1)} %pad_maximum_fusion.16), channel_id=1, replica_groups=mesh['grp'=8,'cy'=4,'cz'=8] {'cz'}, use_global_device_ids=true, to_apply=%region_2.3 | all-reduce | flops 32 | bytes 256 | tf_op jit(solution)/shard_map/psum | solution.py:33
  53.5 10.2 %psum.71 = f32[2,16]{1,0:T(2,128)S(1)} all-reduce(f32[2,16]{1,0:T(2,128)S(1)} %psum.70), channel_id=1, replica_groups=mesh['grp'=8,'cy'=4,'cz'=8] {'cy'}, use_global_device_ids=true, to_apply=%region_3.4 | all-reduce | flops 32 | bytes 256 | tf_op jit(solution)/shard_map/psum | solution.py:33
  65.8 4.0 %collective-permute-start.3 = (f32[16,1,16,128]{3,2,1,0:T(8,128)S(1)}, f32[16,1,16,128]{3,2,1,0:T(8,128)S(1)}, u32[]{:S(2)}, u32[]{:S(2)}) collective-permute-start(f32[16,1,16,128]{3,2,1,0:T(8,128)S(1)} %get-tuple-element.72), channel_id=1, source_target_pairs={{0,1},{1,2},{2,3},{3,4},{4,5},{5,6},{6,7},{7,8},{8,9},{9,10},{10,1... | collective-permute-start | bytes 393224 | tf_op jit(solution)/shard_map/ppermute | solution.py:193
  69.8 2.0 multiply_multiply_fusion.10
  76.6 14.2 %psum.72 = f32[3,16]{1,0:T(4,128)S(1)} all-reduce(f32[3,16]{1,0:T(4,128)S(1)} %pad_maximum_fusion.14), channel_id=1, replica_groups=mesh['grp'=8,'cy'=4,'cz'=8] {'cz'}, use_global_device_ids=true, to_apply=%region_7.8 | all-reduce | flops 48 | bytes 384 | tf_op jit(solution)/shard_map/psum | solution.py:33
  90.8 6.0 %psum.73 = f32[3,16]{1,0:T(4,128)S(1)} all-reduce(f32[3,16]{1,0:T(4,128)S(1)} %psum.72), channel_id=1, replica_groups=mesh['grp'=8,'cy'=4,'cz'=8] {'cy'}, use_global_device_ids=true, to_apply=%region_8.9 | all-reduce | flops 48 | bytes 384 | tf_op jit(solution)/shard_map/psum | solution.py:33
  97.5 2.6 multiply_subtract_fusion.1
  101.7 4.2 %collective-permute-start.5 = (f32[16,1,16,128]{3,2,1,0:T(8,128)S(1)}, f32[16,1,16,128]{3,2,1,0:T(8,128)S(1)}, u32[]{:S(2)}, u32[]{:S(2)}) collective-permute-start(f32[16,1,16,128]{3,2,1,0:T(8,128)S(1)} %get-tuple-element.70), channel_id=1, source_target_pairs={{0,1},{1,2},{2,3},{3,4},{4,5},{5,6},{6,7},{7,8},{8,9},{9,10},{10,1... | collective-permute-start | bytes 393224 | tf_op jit(solution)/shard_map/ppermute | solution.py:193
  105.9 2.0 multiply_multiply_fusion.9
  112.2 14.7 %psum.74 = f32[4,16]{1,0:T(4,128)} all-reduce(f32[4,16]{1,0:T(4,128)S(1)} %pad_maximum_fusion.15), channel_id=1, replica_groups=mesh['grp'=8,'cy'=4,'cz'=8] {'cz'}, use_global_device_ids=true, to_apply=%region_13.14 | all-reduce | flops 64 | bytes 512 | tf_op jit(solution)/shard_map/psum | solution.py:33
  126.9 7.5 %psum.75 = f32[4,16]{1,0:T(4,128)} all-reduce(f32[4,16]{1,0:T(4,128)} %psum.74), channel_id=1, replica_groups=mesh['grp'=8,'cy'=4,'cz'=8] {'cy'}, use_global_device_ids=true, to_apply=%region_14.15 | all-reduce | flops 64 | bytes 512 | tf_op jit(solution)/shard_map/psum | solution.py:33
  136.1 2.4 copy_subtract_fusion
  140.4 4.0 %collective-permute-start.7 = (f32[16,1,16,128]{3,2,1,0:T(8,128)S(1)}, f32[16,1,16,128]{3,2,1,0:T(8,128)S(1)}, u32[]{:S(2)}, u32[]{:S(2)}) collective-permute-start(f32[16,1,16,128]{3,2,1,0:T(8,128)S(1)} %get-tuple-element.68), channel_id=1, source_target_pairs={{0,1},{1,2},{2,3},{3,4},{4,5},{5,6},{6,7},{7,8},{8,9},{9,10},{10,1... | collective-permute-start | bytes 393224 | tf_op jit(solution)/shard_map/ppermute | solution.py:193
  149.7 14.1 %psum.76 = f32[5,16]{1,0:T(8,128)S(1)} all-reduce(f32[5,16]{1,0:T(8,128)S(1)} %stack.169), channel_id=1, replica_groups=mesh['grp'=8,'cy'=4,'cz'=8] {'cz'}, use_global_device_ids=true, to_apply=%region_20.21 | all-reduce | flops 80 | bytes 640 | tf_op jit(solution)/shard_map/psum | solution.py:33
  163.8 7.9 %psum.77 = f32[5,16]{1,0:T(8,128)S(1)} all-reduce(f32[5,16]{1,0:T(8,128)S(1)} %psum.76), channel_id=1, replica_groups=mesh['grp'=8,'cy'=4,'cz'=8] {'cy'}, use_global_device_ids=true, to_apply=%region_21.22 | all-reduce | flops 80 | bytes 640 | tf_op jit(solution)/shard_map/psum | solution.py:33
  171.7 2.3 multiply_reduce_fusion.1
  174.0 12.3 %psum.78 = f32[16]{0:T(128)S(1)} all-reduce(f32[16]{0:T(128)S(1)} %multiply_reduce_fusion.1), channel_id=1, replica_groups=mesh['grp'=8,'cy'=4,'cz'=8] {'cz'}, use_global_device_ids=true, to_apply=%region_23.24 | all-reduce | flops 16 | bytes 128 | tf_op jit(solution)/shard_map/psum | solution.py:33
  186.3 6.1 %psum.79 = f32[16]{0:T(128)S(1)} all-reduce(f32[16]{0:T(128)S(1)} %psum.78), channel_id=1, replica_groups=mesh['grp'=8,'cy'=4,'cz'=8] {'cy'}, use_global_device_ids=true, to_apply=%region_24.25 | all-reduce | flops 16 | bytes 128 | tf_op jit(solution)/shard_map/psum | solution.py:33
  192.6 2.1 multiply_add_fusion
  197.8 2.5 collective-permute-done.8
  200.3 3.5 %collective-permute-done.9 = f32[16,256]{1,0:T(8,128)S(1)} collective-permute-done((f32[16,256]{1,0:T(8,128)S(1)}, f32[16,256]{1,0:T(8,128)S(1)}, u32[]{:S(2)}, u32[]{:S(2)}) %collective-permute-start.9) | collective-permute-done | bytes 16416 | tf_op jit(solution)/shard_map/ppermute | solution.py:37
  203.8 2.3 collective-permute-start.10
  206.0 4.4 %collective-permute-done.10 = f32[16,256]{1,0:T(8,128)S(1)} collective-permute-done((f32[16,256]{1,0:T(8,128)S(1)}, f32[16,256]{1,0:T(8,128)S(1)}, u32[]{:S(2)}, u32[]{:S(2)}) %collective-permute-start.10) | collective-permute-done | bytes 16416 | tf_op jit(solution)/shard_map/ppermute | solution.py:37
  213.9 3.2 %collective-permute-done.12 = f32[16,256]{1,0:T(8,128)S(1)} collective-permute-done((f32[16,256]{1,0:T(8,128)S(1)}, f32[16,256]{1,0:T(8,128)S(1)}, u32[]{:S(2)}, u32[]{:S(2)}) %collective-permute-start.12) | collective-permute-done | bytes 16416 | tf_op jit(solution)/shard_map/ppermute | solution.py:37
  217.1 38.6 %collective-permute-start.13 = (f32[16,256]{1,0:T(8,128)S(1)}, f32[16,256]{1,0:T(8,128)S(1)}, u32[]{:S(2)}, u32[]{:S(2)}) collective-permute-start(f32[16,256]{1,0:T(8,128)S(1)} %add.491), channel_id=1, source_target_pairs={{0,32},{32,64},{64,96},{96,128},{128,160},{160,192},{192,224},{224... | collective-permute-start | bytes 49160 | tf_op jit(solution)/shard_map/ppermute | solution.py:22
  256.6 2.3 collective-permute-start.14
  259.7 2.3 collective-permute-start.15
  265.5 2.3 collective-permute-start.19
  269.2 11.7 %cholesky.17 = f32[128,128]{1,0:T(8,128)S(1)} custom-call(f32[128,128]{1,0:T(8,128)S(1)} %fusion.71), custom_call_target="Cholesky" | custom-call | tf_op jit(solution)/shard_map/jit(cholesky)/cholesky | solution.py:151
  282.3 9.8 %custom-call.10 = f32[1,128,128]{1,2,0:T(8,128)S(1)} custom-call(f32[1,128,128]{2,1,0:T(8,128)S(1)} %fusion.65), custom_call_target="InvertDiagBlocksLowerTriangular" | custom-call | tf_op jit(solution)/shard_map/jit(_cho_solve)/triangular_solve | solution.py:152
  293.6 7.1 %fusion = f32[2,8,128,128]{3,1,2,0:T(8,128)S(1)} fusion(f32[128,16]{1,0:T(8,128)S(1)} %fusion.66, f32[128,16384]{1,0:T(8,128)} %all-gather.2.cloned.1.call-done, f32[2,8,128,128]{3,2,1,0:T(8,128)S(1)} %bitcast.504), kind=kOutput, calls=%fused_computation.3 | convolution fusion | flops 402915328 | bytes 10493952 | tf_op jit(solution)/shard_map/dot_general | solution.py:279
  (286 shorter events, 60.6 us)
Async XLA Ops:
  7.2 286.4 %all-gather.2.cloned.1.call-start = ((), (), s32[]{:S(2)}) async-start(), calls=%async_computation | async-start | bytes 9437184 | tf_op jit(solution)/shard_map/all_gather | solution.py:281
  11.3 15.3 %collective-permute-start.1 = (f32[16,3,1,16,128]{4,3,0,2,1:T(8,128)}, f32[16,3,1,16,128]{4,3,0,2,1:T(8,128)S(1)}, u32[]{:S(2)}, u32[]{:S(2)}) collective-permute-start(f32[16,3,1,16,128]{4,3,0,2,1:T(8,128)} %pad_maximum_fusion.13), channel_id=1, source_target_pairs={{1,0},{2,1},{3,2},{4,3},{5,4},{6,5},{7,6},{8,7},{9,8},{10,9},{11,1... | collective-permute-start | bytes 1179656 | tf_op jit(solution)/shard_map/ppermute | solution.py:177
  13.3 13.3 %collective-permute-start = (f32[16,3,1,16,128]{4,3,0,2,1:T(8,128)}, f32[16,3,1,16,128]{4,3,0,2,1:T(8,128)S(1)}, u32[]{:S(2)}, u32[]{:S(2)}) collective-permute-start(f32[16,3,1,16,128]{4,3,0,2,1:T(8,128)} %pad_maximum_fusion.12), channel_id=1, source_target_pairs={{0,1},{1,2},{2,3},{3,4},{4,5},{5,6},{6,7},{7,8},{8,9},{9,10},{10,1... | collective-permute-start | bytes 1179656 | tf_op jit(solution)/shard_map/ppermute | solution.py:176
  25.8 80.1 %copy-start.43 = (f32[128]{0:T(128)}, f32[128]{0:T(128)S(1)}, u32[]{:S(2)}) copy-start(f32[128]{0:T(128)S(1)} %compare_convert_fusion) | copy-start | bytes 1540
  25.8 80.1 %copy-start.44 = (f32[16]{0:T(128)}, f32[16]{0:T(128)S(1)}, u32[]{:S(2)}) copy-start(f32[16]{0:T(128)S(1)} %compare_convert_fusion.1) | copy-start | bytes 196
  64.4 9.1 %collective-permute-start.2 = (f32[16,1,16,128]{3,2,1,0:T(8,128)S(1)}, f32[16,1,16,128]{3,2,1,0:T(8,128)S(1)}, u32[]{:S(2)}, u32[]{:S(2)}) collective-permute-start(f32[16,1,16,128]{3,2,1,0:T(8,128)S(1)} %get-tuple-element.71), channel_id=1, source_target_pairs={{1,0},{2,1},{3,2},{4,3},{5,4},{6,5},{7,6},{8,7},{9,8},{10,9},{11,1... | collective-permute-start | bytes 393224 | tf_op jit(solution)/shard_map/ppermute | solution.py:194
  65.8 7.7 %collective-permute-start.3 = (f32[16,1,16,128]{3,2,1,0:T(8,128)S(1)}, f32[16,1,16,128]{3,2,1,0:T(8,128)S(1)}, u32[]{:S(2)}, u32[]{:S(2)}) collective-permute-start(f32[16,1,16,128]{3,2,1,0:T(8,128)S(1)} %get-tuple-element.72), channel_id=1, source_target_pairs={{0,1},{1,2},{2,3},{3,4},{4,5},{5,6},{6,7},{7,8},{8,9},{9,10},{10,1... | collective-permute-start | bytes 393224 | tf_op jit(solution)/shard_map/ppermute | solution.py:193
  100.4 8.0 %collective-permute-start.4 = (f32[16,1,16,128]{3,2,1,0:T(8,128)S(1)}, f32[16,1,16,128]{3,2,1,0:T(8,128)S(1)}, u32[]{:S(2)}, u32[]{:S(2)}) collective-permute-start(f32[16,1,16,128]{3,2,1,0:T(8,128)S(1)} %get-tuple-element.69), channel_id=1, source_target_pairs={{1,0},{2,1},{3,2},{4,3},{5,4},{6,5},{7,6},{8,7},{9,8},{10,9},{11,1... | collective-permute-start | bytes 393224 | tf_op jit(solution)/shard_map/ppermute | solution.py:194
  101.7 6.7 %collective-permute-start.5 = (f32[16,1,16,128]{3,2,1,0:T(8,128)S(1)}, f32[16,1,16,128]{3,2,1,0:T(8,128)S(1)}, u32[]{:S(2)}, u32[]{:S(2)}) collective-permute-start(f32[16,1,16,128]{3,2,1,0:T(8,128)S(1)} %get-tuple-element.70), channel_id=1, source_target_pairs={{0,1},{1,2},{2,3},{3,4},{4,5},{5,6},{6,7},{7,8},{8,9},{9,10},{10,1... | collective-permute-start | bytes 393224 | tf_op jit(solution)/shard_map/ppermute | solution.py:193
  139.0 7.1 %collective-permute-start.6 = (f32[16,1,16,128]{3,2,1,0:T(8,128)S(1)}, f32[16,1,16,128]{3,2,1,0:T(8,128)S(1)}, u32[]{:S(2)}, u32[]{:S(2)}) collective-permute-start(f32[16,1,16,128]{3,2,1,0:T(8,128)S(1)} %get-tuple-element.67), channel_id=1, source_target_pairs={{1,0},{2,1},{3,2},{4,3},{5,4},{6,5},{7,6},{8,7},{9,8},{10,9},{11,1... | collective-permute-start | bytes 393224 | tf_op jit(solution)/shard_map/ppermute | solution.py:194
  140.4 5.9 %collective-permute-start.7 = (f32[16,1,16,128]{3,2,1,0:T(8,128)S(1)}, f32[16,1,16,128]{3,2,1,0:T(8,128)S(1)}, u32[]{:S(2)}, u32[]{:S(2)}) collective-permute-start(f32[16,1,16,128]{3,2,1,0:T(8,128)S(1)} %get-tuple-element.68), channel_id=1, source_target_pairs={{0,1},{1,2},{2,3},{3,4},{4,5},{5,6},{6,7},{7,8},{8,9},{9,10},{10,1... | collective-permute-start | bytes 393224 | tf_op jit(solution)/shard_map/ppermute | solution.py:193
  148.2 44.2 %copy-start.42 = (f32[4,16]{1,0:T(4,128)S(1)}, f32[4,16]{1,0:T(4,128)}, u32[]{:S(2)}) copy-start(f32[4,16]{1,0:T(4,128)} %psum.75) | copy-start | bytes 772
  148.2 44.2 %copy-start.46 = (f32[3,16]{1,0:T(4,128)S(1)}, f32[3,16]{1,0:T(4,128)}, u32[]{:S(2)}) copy-start(f32[3,16]{1,0:T(4,128)} %copy-done.45) | copy-start | bytes 580
  148.3 44.2 %copy-start.48 = (f32[2,16]{1,0:T(2,128)S(1)}, f32[2,16]{1,0:T(2,128)}, u32[]{:S(2)}) copy-start(f32[2,16]{1,0:T(2,128)} %copy-done.47) | copy-start | bytes 388
  148.3 44.2 %copy-start.50 = (f32[16]{0:T(128)S(1)}, f32[16]{0:T(128)}, u32[]{:S(2)}) copy-start(f32[16]{0:T(128)} %copy-done.49) | copy-start | bytes 196
  148.3 44.2 %copy-start.52 = (f32[16]{0:T(128)S(1)}, f32[16]{0:T(128)}, u32[]{:S(2)}) copy-start(f32[16]{0:T(128)} %copy-done.51) | copy-start | bytes 196
  148.3 44.2 %copy-start.55 = (f32[16]{0:T(128)S(1)}, f32[16]{0:T(128)}, u32[]{:S(2)}) copy-start(f32[16]{0:T(128)} %get-tuple-element.97) | copy-start | bytes 196
  174.0 91.2 %copy-start.56 = (f32[256]{0:T(256)S(1)}, f32[256]{0:T(256)}, u32[]{:S(2)}) copy-start(f32[256]{0:T(256)} %param.16) | copy-start | bytes 3076
  192.6 99.5 %copy-start.57 = (f32[256]{0:T(256)S(1)}, f32[256]{0:T(256)}, u32[]{:S(2)}) copy-start(f32[256]{0:T(256)} %param.15) | copy-start | bytes 3076
  194.7 98.9 %copy-start.24 = (f32[16,2,4,16,128]{4,3,2,1,0:T(8,128)S(1)}, f32[16,2,4,16,128]{4,3,2,1,0:T(8,128)}, u32[]{:S(2)}) copy-start(f32[16,2,4,16,128]{4,3,2,1,0:T(8,128)} %copy-done.23) | copy-start | bytes 3145732
  197.6 2.7 collective-permute-start.8
  200.3 3.5 %collective-permute-start.9 = (f32[16,256]{1,0:T(8,128)S(1)}, f32[16,256]{1,0:T(8,128)S(1)}, u32[]{:S(2)}, u32[]{:S(2)}) collective-permute-start(f32[16,256]{1,0:T(8,128)S(1)} %add.487), channel_id=1, source_target_pairs={{0,2},{1,3},{2,0},{3,1},{4,6},{5,7},{6,4},{7,5},{8,10},{9,11},{10,... | collective-permute-start | bytes 49160 | tf_op jit(solution)/shard_map/ppermute | solution.py:37
  203.8 6.7 %collective-permute-start.10 = (f32[16,256]{1,0:T(8,128)S(1)}, f32[16,256]{1,0:T(8,128)S(1)}, u32[]{:S(2)}, u32[]{:S(2)}) collective-permute-start(f32[16,256]{1,0:T(8,128)S(1)} %add.488), channel_id=1, source_target_pairs={{0,4},{1,5},{2,6},{3,7},{4,0},{5,1},{6,2},{7,3},{8,12},{9,13},{10,... | collective-permute-start | bytes 49160 | tf_op jit(solution)/shard_map/ppermute | solution.py:37
  210.4 2.6 collective-permute-start.11
  213.0 4.1 %collective-permute-start.12 = (f32[16,256]{1,0:T(8,128)S(1)}, f32[16,256]{1,0:T(8,128)S(1)}, u32[]{:S(2)}, u32[]{:S(2)}) collective-permute-start(f32[16,256]{1,0:T(8,128)S(1)} %add.490), channel_id=1, source_target_pairs={{0,16},{8,24},{16,0},{24,8},{1,17},{9,25},{17,1},{25,9},{2,18},{10... | collective-permute-start | bytes 49160 | tf_op jit(solution)/shard_map/ppermute | solution.py:37
  217.1 39.4 %collective-permute-start.13 = (f32[16,256]{1,0:T(8,128)S(1)}, f32[16,256]{1,0:T(8,128)S(1)}, u32[]{:S(2)}, u32[]{:S(2)}) collective-permute-start(f32[16,256]{1,0:T(8,128)S(1)} %add.491), channel_id=1, source_target_pairs={{0,32},{32,64},{64,96},{96,128},{128,160},{160,192},{192,224},{224... | collective-permute-start | bytes 49160 | tf_op jit(solution)/shard_map/ppermute | solution.py:22
  256.6 3.2 %collective-permute-start.14 = (f32[16,256]{1,0:T(8,128)S(1)}, f32[16,256]{1,0:T(8,128)S(1)}, u32[]{:S(2)}, u32[]{:S(2)}) collective-permute-start(f32[16,256]{1,0:T(8,128)S(1)} %collective-permute-done.13), channel_id=1, source_target_pairs={{0,32},{32,64},{64,96},{96,128},{128,160},{160,192},{192,224},{224... | collective-permute-start | bytes 49160 | tf_op jit(solution)/shard_map/ppermute | solution.py:22
  258.9 3.5 %collective-permute-start.17 = (f32[16,256]{1,0:T(8,128)S(1)}, f32[16,256]{1,0:T(8,128)S(1)}, u32[]{:S(2)}, u32[]{:S(2)}) collective-permute-start(f32[16,256]{1,0:T(8,128)S(1)} %add.491), channel_id=1, source_target_pairs={{0,224},{32,0},{64,32},{96,64},{128,96},{160,128},{192,160},{224,1... | collective-permute-start | bytes 49160 | tf_op jit(solution)/shard_map/ppermute | solution.py:24
  259.7 4.3 %collective-permute-start.15 = (f32[16,256]{1,0:T(8,128)S(1)}, f32[16,256]{1,0:T(8,128)S(1)}, u32[]{:S(2)}, u32[]{:S(2)}) collective-permute-start(f32[16,256]{1,0:T(8,128)S(1)} %collective-permute-done.14), channel_id=1, source_target_pairs={{0,32},{32,64},{64,96},{96,128},{128,160},{160,192},{192,224},{224... | collective-permute-start | bytes 49160 | tf_op jit(solution)/shard_map/ppermute | solution.py:22
  262.3 3.2 %collective-permute-start.18 = (f32[16,256]{1,0:T(8,128)S(1)}, f32[16,256]{1,0:T(8,128)S(1)}, u32[]{:S(2)}, u32[]{:S(2)}) collective-permute-start(f32[16,256]{1,0:T(8,128)S(1)} %collective-permute-done.17), channel_id=1, source_target_pairs={{0,224},{32,0},{64,32},{96,64},{128,96},{160,128},{192,160},{224,1... | collective-permute-start | bytes 49160 | tf_op jit(solution)/shard_map/ppermute | solution.py:24
  264.0 4.4 %collective-permute-start.16 = (f32[16,256]{1,0:T(8,128)S(1)}, f32[16,256]{1,0:T(8,128)S(1)}, u32[]{:S(2)}, u32[]{:S(2)}) collective-permute-start(f32[16,256]{1,0:T(8,128)S(1)} %collective-permute-done.15), channel_id=1, source_target_pairs={{0,32},{32,64},{64,96},{96,128},{128,160},{160,192},{192,224},{224... | collective-permute-start | bytes 49160 | tf_op jit(solution)/shard_map/ppermute | solution.py:22
  265.5 3.2 %collective-permute-start.19 = (f32[16,256]{1,0:T(8,128)S(1)}, f32[16,256]{1,0:T(8,128)S(1)}, u32[]{:S(2)}, u32[]{:S(2)}) collective-permute-start(f32[16,256]{1,0:T(8,128)S(1)} %collective-permute-done.18), channel_id=1, source_target_pairs={{0,224},{32,0},{64,32},{96,64},{128,96},{160,128},{192,160},{224,1... | collective-permute-start | bytes 49160 | tf_op jit(solution)/shard_map/ppermute | solution.py:24
  (47 other events, 476.0 us)
Sparse Core Ops, SparseCore 0:
  22.7 56.6 all-gather.1
